TPU v7x, 256 devices: a whole 4x4x8 slice. The times are simulated.
256 devices in a mesh: ctx: 32 (over y, x, core), head: 8 (over z).
Axes of the slice: x: 4, y: 4, z: 8, core: 2. Of those that a mesh axis runs over, the one named last changes fastest.
Arguments:
- queries: bfloat16 [8192, 4096], P('ctx', 'head'), may hold values from -6 to 6
- key_rows: bfloat16 [8192, 4096], P('ctx', 'head'), may hold values from -6 to 6
- values: bfloat16 [8192, 4096], P('ctx', 'head'), may hold values from -6 to 6
- log_decay: float32 [8192, 32], P('ctx', 'head'), may hold values from 0 to 1, as said below
- head_gain: bfloat16 [4096], P('head'), may hold values from 0.099609375 to 1.8984375
- out_weight: bfloat16 [3072, 4096], P('ctx', 'head'), may hold values from -0.09375 to 0.09375
- residual: bfloat16 [8192, 3072], P('ctx', 'head'), may hold values from -6 to 6
- norm_gain: bfloat16 [3072], P('head'), may hold values from 0.099609375 to 1.8984375
- router: bfloat16 [3072, 32], replicated, may hold values from -0.21875 to 0.21875
- expert_ids: int32 [8192, 2], P('ctx'), may hold values from 0 to 31, all different within a row; in each aligned block of 256 rows (0 to 255, 256 to 511, ...) at most 24 rows name the same one
- gate_weight: bfloat16 [32, 3072, 5120], P('ctx', None, 'head'), may hold values from -0.109375 to 0.109375
- up_weight: bfloat16 [32, 3072, 5120], P('ctx', None, 'head'), may hold values from -0.109375 to 0.109375
- down_weight: bfloat16 [32, 5120, 3072], P('ctx', 'head'), may hold values from -0.125 to 0.125
Outputs:
- layer_out: float32 [8192, 3072], P('ctx', 'head')
Inputs may be any that keep to these rules, and one draw needn't show every extreme that they name: `log_decay`: amounts by which a head's state decays at a position: the state is multiplied by exp(-value). `expert_ids`: each row names 2 different experts; among the rows of one block of 256 positions no expert is named more than 24 times, a bound that some block reaches.
All inputs are finite; a program needn't handle non-finite values.
Results may differ from a plain program's by a relative error of at most 0.007.
Values may be sent and summed in bfloat16 or wider, within the bound.
No kernel may reach another device: no remote copies, remote signals or barrier semaphores. Data moves between devices by JAX's collectives and lax.ppermute only.
A program may use at most 128 MiB of HBM per device.

v0:
```python
import jax
import jax.numpy as jnp
from jax import lax
from jax.sharding import PartitionSpec as P

HEAD_DIM = 128
TOP = 2
HIGH = lax.Precision.HIGHEST
EPSILON = 1e-05


def combine(earlier, later):
    rows = HEAD_DIM
    decay_late = later[:, rows : rows + 1, 0:1]
    state = decay_late * earlier[:, :rows] + later[:, :rows]
    decay = earlier[:, rows : rows + 1] * later[:, rows : rows + 1]
    pad = jnp.zeros((later.shape[0], later.shape[1] - rows - 1, later.shape[2]), later.dtype)
    return jnp.concatenate([state, decay, pad], axis=1)


def exclusive_scan(packed, axis):
    count, mine = (lax.axis_size(axis), lax.axis_index(axis))
    rows = HEAD_DIM
    identity = jnp.zeros_like(packed).at[:, rows].set(1.0)
    window = packed
    before = identity
    base = 1
    while base < count:
        joined = None
        for step in range(1, 4):
            shift = step * base
            if shift >= count:
                break
            pairs = [(j, j + shift) for j in range(count - shift)]
            got = lax.ppermute(window, axis, pairs)
            got = jnp.where(mine >= shift, got, identity)
            joined = got if joined is None else combine(got, joined)
        before = combine(joined, before)
        if 4 * base < count:
            window = combine(joined, window)
        base *= 4
    return before[:, :rows]


def on_device(
    queries,
    key_rows,
    values,
    log_decay,
    head_gain,
    out_weight,
    residual,
    norm_gain,
    router,
    expert_ids,
    gate_weight,
    up_weight,
    down_weight,
):
    rows = queries.shape[0]
    heads_here = log_decay.shape[1]
    groups = lax.axis_size("head")
    query_heads = queries.reshape(rows, heads_here, HEAD_DIM)
    key_heads = key_rows.reshape(rows, heads_here, HEAD_DIM)
    value_heads = values.reshape(rows, heads_here, HEAD_DIM)
    cumulative = jnp.cumsum(log_decay, axis=0)
    scores = jnp.einsum("thd,jhd->htj", query_heads, key_heads, preferred_element_type=jnp.float32)
    causal = jnp.arange(rows)[:, None] >= jnp.arange(rows)[None, :]
    gap = cumulative.T[:, :, None] - cumulative.T[:, None, :]
    weight = jnp.where(causal[None], jnp.exp(-jnp.where(causal[None], gap, 0.0)), 0.0)
    weighted = (scores * weight).astype(jnp.bfloat16)
    inner = jnp.einsum("htj,jhd->thd", weighted, value_heads, preferred_element_type=jnp.float32)
    value_wide = value_heads.astype(jnp.float32)
    tail = jnp.exp(cumulative - cumulative[-1:])
    keys_tail = key_heads.astype(jnp.float32) * tail[:, :, None]
    local_state = jnp.einsum("jhd,jhe->hde", keys_tail, value_wide, precision=HIGH)
    shard_decay = jnp.exp(-cumulative[-1])
    decay_rows = jnp.broadcast_to(shard_decay[:, None, None], (heads_here, 1, HEAD_DIM))
    pad = jnp.zeros((heads_here, 7, HEAD_DIM), jnp.float32)
    packed = jnp.concatenate([local_state, decay_rows, pad], axis=1)
    incoming = exclusive_scan(packed, "ctx")
    query_decayed = query_heads.astype(jnp.float32) * jnp.exp(-cumulative)[:, :, None]
    outer = jnp.einsum("thd,hde->the", query_decayed, incoming, precision=HIGH)
    mixed = inner + outer
    mean_sq = jnp.mean(mixed * mixed, axis=-1, keepdims=True)
    gain_heads = head_gain.astype(jnp.float32).reshape(heads_here, HEAD_DIM)
    normed = (
        (mixed * lax.rsqrt(mean_sq + EPSILON) * gain_heads)
        .astype(jnp.bfloat16)
        .reshape(rows, heads_here * HEAD_DIM)
    )
    width = residual.shape[1]
    full = width * groups
    weight_all = lax.all_gather(out_weight, "ctx", axis=0, tiled=True).reshape(
        groups, width, heads_here * HEAD_DIM
    )
    partial_proj = jnp.einsum("tk,gck->gtc", normed, weight_all, preferred_element_type=jnp.float32)
    total = lax.psum_scatter(partial_proj, "head", scatter_dimension=0, tiled=True)
    stream_mine = residual.astype(jnp.float32) + total[0]
    sq_part = jnp.sum(stream_mine * stream_mine, axis=1)
    sq_hi = sq_part.astype(jnp.bfloat16)
    sq_lo = (sq_part - sq_hi.astype(jnp.float32)).astype(jnp.bfloat16)
    extra = jnp.zeros((8, width), jnp.bfloat16)
    extra = extra.at[0].set(norm_gain)
    extra = extra.at[1, :rows].set(sq_hi)
    extra = extra.at[2, :rows].set(sq_lo)
    payload = jnp.concatenate([stream_mine.astype(jnp.bfloat16), extra], axis=0)
    gathered = lax.all_gather(payload, "head", axis=1, tiled=True)
    stream_wide = gathered[:rows].astype(jnp.float32)
    gain_full = gathered[rows].astype(jnp.float32)
    sq_parts = gathered[rows + 1 : rows + 3].astype(jnp.float32).reshape(2, groups, width)
    stream_sq = jnp.sum(sq_parts[:, :, :rows], axis=(0, 1))[:, None] / full
    moe_in = (stream_wide * lax.rsqrt(stream_sq + EPSILON) * gain_full).astype(jnp.bfloat16)
    experts = router.shape[1]
    capacity = 3 * rows * TOP // (2 * experts)
    logits = jnp.dot(moe_in, router, preferred_element_type=jnp.float32)
    picked_mask = expert_ids[:, :, None] == jnp.arange(experts, dtype=jnp.int32)[None, None, :]
    picked = jnp.sum(jnp.where(picked_mask, logits[:, None, :], 0.0), axis=-1)
    mix_weights = jax.nn.sigmoid(picked - picked[:, ::-1])
    flat_ids = expert_ids.reshape(-1)
    onehot = (flat_ids[:, None] == jnp.arange(experts, dtype=jnp.int32)[None, :]).astype(jnp.int32)
    before = jnp.cumsum(onehot, axis=0) - onehot
    position = jnp.sum(before * onehot, axis=1)
    slot = flat_ids * capacity + position
    owner = jnp.arange(rows * TOP, dtype=jnp.int32) // TOP
    slot_token = jnp.zeros((experts * capacity,), jnp.int32).at[slot].set(owner)
    filled = jnp.zeros((experts * capacity,), jnp.bool_).at[slot].set(True)
    blank = jnp.zeros((), jnp.bfloat16)
    outgoing = jnp.where(filled[:, None], moe_in[slot_token], blank).reshape(
        experts, capacity, full
    )
    half = capacity // 2
    down = down_weight[0].reshape(down_weight.shape[1], groups, width)
    parts = []
    for lo, hi in ((0, half), (half, capacity)):
        arriving = lax.all_to_all(
            outgoing[:, lo:hi], "ctx", split_axis=0, concat_axis=0, tiled=True
        )
        flat = arriving.reshape(-1, full)
        gate = jnp.dot(flat, gate_weight[0], preferred_element_type=jnp.float32)
        up = jnp.dot(flat, up_weight[0], preferred_element_type=jnp.float32)
        activated = (jax.nn.silu(gate) * up).astype(jnp.bfloat16)
        partial_value = jnp.einsum(
            "rf,fgc->grc", activated, down, preferred_element_type=jnp.float32
        ).astype(jnp.bfloat16)
        summed = lax.psum_scatter(partial_value, "head", scatter_dimension=0, tiled=True)
        summed = summed.reshape(arriving.shape[0], arriving.shape[1], width)
        parts.append(lax.all_to_all(summed, "ctx", split_axis=0, concat_axis=0, tiled=True))
    returned = jnp.concatenate(parts, axis=1)
    picked_rows = returned.reshape(experts * capacity, width)[slot].astype(jnp.float32)
    moe_out = jnp.sum(picked_rows.reshape(rows, TOP, width) * mix_weights[:, :, None], axis=1)
    return stream_mine + moe_out


def solution(mesh):
    placed = (
        P("ctx", "head"),
        P("ctx", "head"),
        P("ctx", "head"),
        P("ctx", "head"),
        P("head"),
        P("ctx", "head"),
        P("ctx", "head"),
        P("head"),
        P(),
        P("ctx", None),
        P("ctx", None, "head"),
        P("ctx", None, "head"),
        P("ctx", "head", None),
    )
    return jax.shard_map(
        on_device, mesh=mesh, in_specs=placed, out_specs=P("ctx", "head"), check_vma=False
    )
```

profile of v0, /device:TPU:1, one launch (start us, length us, event | category | flops | bytes accessed | tf_op | source)
XLA Modules:
  0.0 394.2 jit_solution(11019015704431273449)
XLA Ops:
  13.1 6.0 %collective-permute-start.2 = (f32[4,136,128]{2,1,0:T(8,128)S(1)}, f32[4,136,128]{2,1,0:T(8,128)S(1)}, u32[]{:S(2)}, u32[]{:S(2)}) collective-permute-start(f32[4,136,128]{2,1,0:T(8,128)S(1)} %maximum_maximum_fusion), channel_id=1, source_target_pairs={{0,24},{8,32},{16,40},{24,48},{32,56},{40,64},{48,72},{56,80},{64,... | collective-permute-start | bytes 835592 | tf_op jit(solution)/shard_map/ppermute | solution.py:35
  24.3 6.0 %collective-permute-done.1 = f32[4,136,128]{2,1,0:T(8,128)S(1)} collective-permute-done((f32[4,136,128]{2,1,0:T(8,128)S(1)}, f32[4,136,128]{2,1,0:T(8,128)S(1)}, u32[]{:S(2)}, u32[]{:S(2)}) %collective-permute-start.1) | collective-permute-done | bytes 278560 | tf_op jit(solution)/shard_map/ppermute | solution.py:35
  36.4 5.3 %collective-permute-start.5 = (f32[4,136,128]{2,1,0:T(8,128)S(1)}, f32[4,136,128]{2,1,0:T(8,128)S(1)}, u32[]{:S(2)}, u32[]{:S(2)}) collective-permute-start(f32[4,136,128]{2,1,0:T(8,128)S(1)} %maximum_maximum_fusion.1), channel_id=1, source_target_pairs={{0,32},{8,40},{16,48},{24,56},{32,64},{40,72},{48,80},{56,88},{64,... | collective-permute-start | bytes 835592 | tf_op jit(solution)/shard_map/ppermute | solution.py:35
  44.9 6.0 %collective-permute-start.3 = (f32[4,136,128]{2,1,0:T(8,128)S(1)}, f32[4,136,128]{2,1,0:T(8,128)S(1)}, u32[]{:S(2)}, u32[]{:S(2)}) collective-permute-start(f32[4,136,128]{2,1,0:T(8,128)S(1)} %maximum_maximum_fusion.1), channel_id=1, source_target_pairs={{0,96},{8,104},{16,112},{24,120},{32,128},{40,136},{48,144},{56,15... | collective-permute-start | bytes 835592 | tf_op jit(solution)/shard_map/ppermute | solution.py:35
  52.5 15.9 %collective-permute-done.4 = f32[4,136,128]{2,1,0:T(8,128)S(1)} collective-permute-done((f32[4,136,128]{2,1,0:T(8,128)S(1)}, f32[4,136,128]{2,1,0:T(8,128)S(1)}, u32[]{:S(2)}, u32[]{:S(2)}) %collective-permute-start.4) | collective-permute-done | bytes 278560 | tf_op jit(solution)/shard_map/ppermute | solution.py:35
  69.0 5.8 %collective-permute-start.6 = (f32[4,136,128]{2,1,0:T(8,128)S(1)}, f32[4,136,128]{2,1,0:T(8,128)S(1)}, u32[]{:S(2)}, u32[]{:S(2)}) collective-permute-start(f32[4,136,128]{2,1,0:T(8,128)S(1)} %maximum_maximum_fusion.2), channel_id=1, source_target_pairs={{0,128},{8,136},{16,144},{24,152},{32,160},{40,168},{48,176},{56,1... | collective-permute-start | bytes 835592 | tf_op jit(solution)/shard_map/ppermute | solution.py:35
  76.3 4.3 %collective-permute-done.6 = f32[4,136,128]{2,1,0:T(8,128)S(1)} collective-permute-done((f32[4,136,128]{2,1,0:T(8,128)S(1)}, f32[4,136,128]{2,1,0:T(8,128)S(1)}, u32[]{:S(2)}, u32[]{:S(2)}) %collective-permute-start.6) | collective-permute-done | bytes 278560 | tf_op jit(solution)/shard_map/ppermute | solution.py:35
  82.3 4.6 %convolution_bitcast_fusion = f32[8,256,384]{2,1,0:T(8,128)} fusion(bf16[256,512,1]{0,1,2:T(8,128)(2,1)S(1)} %bitcast.159, bf16[8,384,512]{2,1,0:T(8,128)(2,1)} %bitcast.158), kind=kOutput, calls=%fused_computation.20 | convolution fusion | flops 805306368 | bytes 6553600 | tf_op jit(solution)/shard_map/tk,gck->gtc/dot_general | solution.py:97
  87.6 45.2 %reduce-scatter.4.cloned.1.call-done = f32[1,256,384]{2,1,0:T(8,128)} async-done(((f32[8,256,384]{2,1,0:T(8,128)}), f32[1,256,384]{2,1,0:T(8,128)}) %reduce-scatter.4.cloned.1.call-update) | async-done | bytes 393232 | tf_op jit(solution)/shard_map/reduce_scatter | solution.py:98
  142.7 30.0 %all-gather.5.cloned.1.call-done = bf16[264,3072]{1,0:T(8,128)(2,1)} async-done(((bf16[264,384]{1,0:T(8,128)(2,1)}), bf16[264,3072]{1,0:T(8,128)(2,1)}) %all-gather.5.cloned.1.call-update) | async-done | bytes 1622032 | tf_op jit(solution)/shard_map/all_gather | solution.py:108
  176.3 5.0 %gather_fusion = bf16[768,3072]{1,0:T(8,128)(2,1)} fusion(bf16[256,3072]{1,0:T(8,128)(2,1)S(1)} %multiply_convert_fusion, s32[1024]{0:T(1024)S(1)} %pad_clamp_fusion.1), kind=kCustom, calls=%fused_computation | custom fusion | bytes 9440256 | tf_op jit(solution)/shard_map/gather | solution.py:129
  188.0 12.7 %all-to-all-start.2 = ((bf16[32,12,3072]{2,1,0:T(8,128)(2,1)}), bf16[32,12,3072]{2,1,0:T(8,128)(2,1)}, u32[]{:S(2)}, u32[]{:S(2)}) async-start(bf16[32,12,3072]{2,1,0:T(8,128)(2,1)} %get-tuple-element.66), calls=%async_computation.4 | async-start | bytes 6291456 | tf_op jit(solution)/shard_map/all_to_all | solution.py:136
  200.8 4.9 %copy.111 = bf16[80,8,8,384]{3,2,1,0:T(8,128)(2,1)} copy(bf16[80,8,8,384]{3,1,2,0:T(8,128)(2,1)} %bitcast.155) | data formatting | bytes 7864320
  205.7 34.8 %all-to-all-done.2 = bf16[32,12,3072]{2,1,0:T(8,128)(2,1)} async-done(((bf16[32,12,3072]{2,1,0:T(8,128)(2,1)}), bf16[32,12,3072]{2,1,0:T(8,128)(2,1)}, u32[]{:S(2)}, u32[]{:S(2)}) %all-to-all-start.2) | async-done | bytes 2359328 | tf_op jit(solution)/shard_map/all_to_all | solution.py:136
  240.6 4.2 %reshape.300 = bf16[384,3072]{1,0:T(8,128)(2,1)} reshape(bf16[32,12,3072]{2,1,0:T(8,128)(2,1)} %all-to-all-done.2) | data formatting | bytes 4718592 | tf_op jit(solution)/shard_map/reshape | solution.py:139
  244.8 4.8 %fusion.4 = f32[384,640]{1,0:T(8,128)S(1)} fusion(bf16[384,3072]{1,0:T(8,128)(2,1)} %reshape.300, bf16[1,3072,640]{2,1,0:T(8,128)(2,1)} %param.31), kind=kOutput, calls=%fused_computation.9 | convolution fusion | flops 1509949440 | bytes 7274496 | tf_op jit(solution)/shard_map/dot_general | solution.py:140
  249.6 10.3 %convert_bitcast_fusion = bf16[8,384,384]{2,1,0:T(8,128)(2,1)} fusion(bf16[640,8,384]{2,1,0:T(8,128)(2,1)} %bitcast.156, bf16[384,3072]{1,0:T(8,128)(2,1)} %reshape.300, bf16[1,3072,640]{2,1,0:T(8,128)(2,1)} %param.32, f32[384,640]{1,0:T(8,128)S(1)} %fusion.4), kind=kOutput, calls=%fused_computation.18 | convolution fusion | flops 3022553088 | bytes 13565952 | tf_op jit(solution)/shard_map/rf,fgc->grc/dot_general | solution.py:143
  260.0 46.5 %all_to_all.20 = bf16[32,12,3072]{2,1,0:T(8,128)(2,1)} all-to-all(bf16[32,12,3072]{2,1,0:T(8,128)(2,1)} %get-tuple-element.65), channel_id=1, replica_groups=mesh['ctx'=32,'head'=8] {'ctx'}, dimensions={0} | all-to-all | bytes 4718592 | tf_op jit(solution)/shard_map/all_to_all | solution.py:136
  306.5 4.2 %reshape.298 = bf16[384,3072]{1,0:T(8,128)(2,1)} reshape(bf16[32,12,3072]{2,1,0:T(8,128)(2,1)} %all_to_all.20) | data formatting | bytes 4718592 | tf_op jit(solution)/shard_map/reshape | solution.py:139
  310.8 4.8 %fusion.6 = f32[384,640]{1,0:T(8,128)S(1)} fusion(bf16[384,3072]{1,0:T(8,128)(2,1)} %reshape.298, bf16[1,3072,640]{2,1,0:T(8,128)(2,1)} %param.31), kind=kOutput, calls=%fused_computation.11 | convolution fusion | flops 1509949440 | bytes 7274496 | tf_op jit(solution)/shard_map/dot_general | solution.py:140
  315.6 10.3 %convert_bitcast_fusion.1 = bf16[8,384,384]{2,1,0:T(8,128)(2,1)} fusion(bf16[640,8,384]{2,1,0:T(8,128)(2,1)} %bitcast.157, bf16[384,3072]{1,0:T(8,128)(2,1)} %reshape.298, bf16[1,3072,640]{2,1,0:T(8,128)(2,1)} %param.32, f32[384,640]{1,0:T(8,128)S(1)} %fusion.6), kind=kOutput, calls=%fused_computation.19 | convolution fusion | flops 3022553088 | bytes 13565952 | tf_op jit(solution)/shard_map/rf,fgc->grc/dot_general | solution.py:143
  332.3 27.5 %reduce-scatter.6.cloned.1.call-done = bf16[1,384,384]{2,1,0:T(8,128)(2,1)} async-done(((bf16[8,384,384]{2,1,0:T(8,128)(2,1)}), bf16[1,384,384]{2,1,0:T(8,128)(2,1)}) %reduce-scatter.6.cloned.1.call-update) | async-done | bytes 294928 | tf_op jit(solution)/shard_map/reduce_scatter | solution.py:146
  361.5 11.7 %all-to-all-start.1 = ((bf16[32,12,384]{2,1,0:T(8,128)(2,1)}), bf16[32,12,384]{2,1,0:T(8,128)(2,1)S(1)}, u32[]{:S(2)}, u32[]{:S(2)}) async-start(bf16[32,12,384]{2,1,0:T(8,128)(2,1)} %reshape.299), calls=%async_computation.3 | async-start | bytes 786432 | tf_op jit(solution)/shard_map/all_to_all | solution.py:148
  373.5 9.9 %all-to-all-done.1 = bf16[32,12,384]{2,1,0:T(8,128)(2,1)S(1)} async-done(((bf16[32,12,384]{2,1,0:T(8,128)(2,1)}), bf16[32,12,384]{2,1,0:T(8,128)(2,1)S(1)}, u32[]{:S(2)}, u32[]{:S(2)}) %all-to-all-start.1) | async-done | bytes 294944 | tf_op jit(solution)/shard_map/all_to_all | solution.py:148
  (135 shorter events, 59.4 us)
Async XLA Ops:
  6.5 44.4 %copy-start = (bf16[256,512]{1,0:T(8,128)(2,1)S(1)}, bf16[256,512]{1,0:T(8,128)(2,1)}, u32[]{:S(2)}) copy-start(bf16[256,512]{1,0:T(8,128)(2,1)} %param.21) | copy-start | bytes 786436
  6.5 44.5 %copy-start.5 = (bf16[256,512]{1,0:T(8,128)(2,1)S(1)}, bf16[256,512]{1,0:T(8,128)(2,1)}, u32[]{:S(2)}) copy-start(bf16[256,512]{1,0:T(8,128)(2,1)} %param.23) | copy-start | bytes 786436
  6.5 75.8 %all-gather.3.cloned.1.call-start = ((), (), s32[]{:S(2)}) async-start(), calls=%async_computation.7 | async-start | bytes 3244032 | tf_op jit(solution)/shard_map/all_gather | solution.py:94
  7.3 125.6 %reduce-scatter.4.cloned.1.call-start = ((), (), s32[]{:S(2)}) async-start(), calls=%async_computation.8 | async-start | bytes 3538944 | tf_op jit(solution)/shard_map/reduce_scatter | solution.py:98
  10.8 25.5 %copy-start.10 = (f32[136]{0:T(256)}, f32[136]{0:T(256)S(1)}, u32[]{:S(2)}) copy-start(f32[136]{0:T(256)S(1)} %pad.23.clone) | copy-start | bytes 1636
  13.1 11.2 %collective-permute-start.2 = (f32[4,136,128]{2,1,0:T(8,128)S(1)}, f32[4,136,128]{2,1,0:T(8,128)S(1)}, u32[]{:S(2)}, u32[]{:S(2)}) collective-permute-start(f32[4,136,128]{2,1,0:T(8,128)S(1)} %maximum_maximum_fusion), channel_id=1, source_target_pairs={{0,24},{8,32},{16,40},{24,48},{32,56},{40,64},{48,72},{56,80},{64,... | collective-permute-start | bytes 835592 | tf_op jit(solution)/shard_map/ppermute | solution.py:35
  19.2 11.2 %collective-permute-start.1 = (f32[4,136,128]{2,1,0:T(8,128)S(1)}, f32[4,136,128]{2,1,0:T(8,128)S(1)}, u32[]{:S(2)}, u32[]{:S(2)}) collective-permute-start(f32[4,136,128]{2,1,0:T(8,128)S(1)} %maximum_maximum_fusion), channel_id=1, source_target_pairs={{0,8},{8,16},{16,24},{24,32},{32,40},{40,48},{48,56},{56,64},{64,7... | collective-permute-start | bytes 835592 | tf_op jit(solution)/shard_map/ppermute | solution.py:35
  21.1 13.3 %collective-permute-start = (f32[4,136,128]{2,1,0:T(8,128)S(1)}, f32[4,136,128]{2,1,0:T(8,128)S(1)}, u32[]{:S(2)}, u32[]{:S(2)}) collective-permute-start(f32[4,136,128]{2,1,0:T(8,128)S(1)} %maximum_maximum_fusion), channel_id=1, source_target_pairs={{0,16},{8,24},{16,32},{24,40},{32,48},{40,56},{48,64},{56,72},{64,... | collective-permute-start | bytes 835592 | tf_op jit(solution)/shard_map/ppermute | solution.py:35
  35.4 33.0 %copy-start.2 = (f32[4,136,128]{2,1,0:T(8,128)S(1)}, f32[4,136,128]{2,1,0:T(8,128)}, u32[]{:S(2)}) copy-start(f32[4,136,128]{2,1,0:T(8,128)} %constant.174.clone.1) | copy-start | bytes 835588
  36.0 8.9 %copy-start.7 = (f32[4,1,128]{2,1,0:T(1,128)}, f32[4,1,128]{2,1,0:T(1,128)S(1)}, u32[]{:S(2)}) copy-start(f32[4,1,128]{2,1,0:T(1,128)S(1)} %get-tuple-element.62) | copy-start | bytes 6148
  36.4 16.2 %collective-permute-start.5 = (f32[4,136,128]{2,1,0:T(8,128)S(1)}, f32[4,136,128]{2,1,0:T(8,128)S(1)}, u32[]{:S(2)}, u32[]{:S(2)}) collective-permute-start(f32[4,136,128]{2,1,0:T(8,128)S(1)} %maximum_maximum_fusion.1), channel_id=1, source_target_pairs={{0,32},{8,40},{16,48},{24,56},{32,64},{40,72},{48,80},{56,88},{64,... | collective-permute-start | bytes 835592 | tf_op jit(solution)/shard_map/ppermute | solution.py:35
  41.7 26.7 %collective-permute-start.4 = (f32[4,136,128]{2,1,0:T(8,128)S(1)}, f32[4,136,128]{2,1,0:T(8,128)S(1)}, u32[]{:S(2)}, u32[]{:S(2)}) collective-permute-start(f32[4,136,128]{2,1,0:T(8,128)S(1)} %maximum_maximum_fusion.1), channel_id=1, source_target_pairs={{0,64},{8,72},{16,80},{24,88},{32,96},{40,104},{48,112},{56,120},{... | collective-permute-start | bytes 835592 | tf_op jit(solution)/shard_map/ppermute | solution.py:35
  44.9 23.5 %collective-permute-start.3 = (f32[4,136,128]{2,1,0:T(8,128)S(1)}, f32[4,136,128]{2,1,0:T(8,128)S(1)}, u32[]{:S(2)}, u32[]{:S(2)}) collective-permute-start(f32[4,136,128]{2,1,0:T(8,128)S(1)} %maximum_maximum_fusion.1), channel_id=1, source_target_pairs={{0,96},{8,104},{16,112},{24,120},{32,128},{40,136},{48,144},{56,15... | collective-permute-start | bytes 835592 | tf_op jit(solution)/shard_map/ppermute | solution.py:35
  52.4 16.5 %copy-start.11 = (f32[136]{0:T(256)S(1)}, f32[136]{0:T(256)}, u32[]{:S(2)}) copy-start(f32[136]{0:T(256)} %copy-done.10) | copy-start | bytes 1636
  69.0 11.6 %collective-permute-start.6 = (f32[4,136,128]{2,1,0:T(8,128)S(1)}, f32[4,136,128]{2,1,0:T(8,128)S(1)}, u32[]{:S(2)}, u32[]{:S(2)}) collective-permute-start(f32[4,136,128]{2,1,0:T(8,128)S(1)} %maximum_maximum_fusion.2), channel_id=1, source_target_pairs={{0,128},{8,136},{16,144},{24,152},{32,160},{40,168},{48,176},{56,1... | collective-permute-start | bytes 835592 | tf_op jit(solution)/shard_map/ppermute | solution.py:35
  87.0 45.9 %copy-start.4 = (bf16[256,384]{1,0:T(8,128)(2,1)S(1)}, bf16[256,384]{1,0:T(8,128)(2,1)}, u32[]{:S(2)}) copy-start(bf16[256,384]{1,0:T(8,128)(2,1)} %param.27) | copy-start | bytes 589828
  87.0 48.2 %copy-start.9 = (s32[256,2]{0,1:T(2,128)S(1)}, s32[256,2]{0,1:T(2,128)}, u32[]{:S(2)}) copy-start(s32[256,2]{0,1:T(2,128)} %param.30) | copy-start | bytes 6148
  87.0 85.8 %all-gather.5.cloned.1.call-start = ((), (), s32[]{:S(2)}) async-start(), calls=%async_computation.9 | async-start | bytes 1824768 | tf_op jit(solution)/shard_map/all_gather | solution.py:108
  188.0 52.5 %all-to-all-start.2 = ((bf16[32,12,3072]{2,1,0:T(8,128)(2,1)}), bf16[32,12,3072]{2,1,0:T(8,128)(2,1)}, u32[]{:S(2)}, u32[]{:S(2)}) async-start(bf16[32,12,3072]{2,1,0:T(8,128)(2,1)} %get-tuple-element.66), calls=%async_computation.4 | async-start | bytes 6291456 | tf_op jit(solution)/shard_map/all_to_all | solution.py:136
  200.7 125.2 %reduce-scatter.8.cloned.1.call-start = ((), (), s32[]{:S(2)}) async-start(), calls=%async_computation.11 | async-start | bytes 2654208 | tf_op jit(solution)/shard_map/reduce_scatter | solution.py:146
  259.9 99.8 %reduce-scatter.6.cloned.1.call-start = ((), (), s32[]{:S(2)}) async-start(), calls=%async_computation.10 | async-start | bytes 2654208 | tf_op jit(solution)/shard_map/reduce_scatter | solution.py:146
  325.9 5.8 %copy-start.6 = (bf16[3072,32]{0,1:T(8,128)(2,1)S(1)}, bf16[3072,32]{0,1:T(8,128)(2,1)}, u32[]{:S(2)}) copy-start(bf16[3072,32]{0,1:T(8,128)(2,1)} %param.29) | copy-start | bytes 589828
  327.7 33.8 %all-to-all-start.3 = ((bf16[32,12,384]{2,1,0:T(8,128)(2,1)}), bf16[32,12,384]{2,1,0:T(8,128)(2,1)S(1)}, u32[]{:S(2)}, u32[]{:S(2)}) async-start(bf16[32,12,384]{2,1,0:T(8,128)(2,1)} %reshape.301), calls=%async_computation.6 | async-start | bytes 786432 | tf_op jit(solution)/shard_map/all_to_all | solution.py:148
  361.5 21.8 %all-to-all-start.1 = ((bf16[32,12,384]{2,1,0:T(8,128)(2,1)}), bf16[32,12,384]{2,1,0:T(8,128)(2,1)S(1)}, u32[]{:S(2)}, u32[]{:S(2)}) async-start(bf16[32,12,384]{2,1,0:T(8,128)(2,1)} %reshape.299), calls=%async_computation.3 | async-start | bytes 786432 | tf_op jit(solution)/shard_map/all_to_all | solution.py:148
  (5 other events, 13.0 us)
Sparse Core Ops, SparseCore 0:
  9.9 61.5 all-gather.2
  87.1 45.7 reduce-scatter.3
  135.3 37.3 all-gather.4
  260.0 34.8 reduce-scatter.7
  326.0 33.6 reduce-scatter.5
where the time goes:
time: 395 us; the launch traced here: 394 us
  waiting for transfers between devices  179 us (45%)
  starting transfers between devices  59.1 us (15%)
  blocking collectives  46.5 us (12%)
  matrix products  39.6 us (10%)
  local copies, waits for them, and re-layouts  39.4 us (10%)
  other arithmetic  16.4 us (4%)
  between operations  13.7 us (3%)
    all_to_all x1, blocking collectives, on_device(): lax.all_to_all(outgoing[:, lo:hi], 'ctx', split_axis=0, concat_axis=0, ti...  46.5 us
    reduce_scatter x1, waiting for transfers between devices, on_device(): lax.psum_scatter(partial_proj, 'head', scatter_dimension=0, tiled=True)  45.2 us
    all_to_all x1, waiting for transfers between devices, on_device(): lax.all_to_all(outgoing[:, lo:hi], 'ctx', split_axis=0, concat_axis=0, ti...  34.8 us
    ppermute x7, waiting for transfers between devices, exclusive_scan(): got = lax.ppermute(window, axis, pairs)  31.2 us
    ppermute x7, starting transfers between devices, exclusive_scan(): got = lax.ppermute(window, axis, pairs)  30.6 us
    all_gather x1, waiting for transfers between devices, on_device(): gathered = lax.all_gather(payload, 'head', axis=1, tiled=True)  30 us
    reduce_scatter x2, waiting for transfers between devices, on_device(): lax.psum_scatter(partial_value, 'head', scatter_dimension=0, tiled=True)  27.5 us
    dot_general x2, matrix products, on_device(): jnp.einsum('rf,fgc->grc', activated, down, preferred_element_type=jnp.flo...  20.6 us
  transfers between devices with their start and end apart: 15, of which 10 were waited for; matrix products, arithmetic and copies ran while one was open for 12% of the time, Pallas kernels for 0%

commit v1 on v0

--- a/solution.py
+++ b/solution.py
@@ -105,7 +105,9 @@
     extra = extra.at[1, :rows].set(sq_hi)
     extra = extra.at[2, :rows].set(sq_lo)
     payload = jnp.concatenate([stream_mine.astype(jnp.bfloat16), extra], axis=0)
-    gathered = lax.all_gather(payload, "head", axis=1, tiled=True)
+    gathered = jnp.concatenate(
+        lax.all_to_all(jnp.stack([payload] * lax.axis_size("head")), "head", 0, 0), axis=1
+    )
     stream_wide = gathered[:rows].astype(jnp.float32)
     gain_full = gathered[rows].astype(jnp.float32)
     sq_parts = gathered[rows + 1 : rows + 3].astype(jnp.float32).reshape(2, groups, width)

time: 395 us -> 395 us (level)
    all_to_all x0 -> x1, waiting for transfers between devices: none -> 30.8 us  [on_device(): lax.all_to_all(jnp.stack([payload] * lax.axis_size('head')), 'head', 0, 0)]
    all_gather x1 -> x0, waiting for transfers between devices: 30 us -> none  [on_device(): gathered = lax.all_gather(payload, 'head', axis=1, tiled=True)]
    all_to_all x0 -> x1, starting transfers between devices: none -> 4.98 us  [on_device(): lax.all_to_all(jnp.stack([payload] * lax.axis_size('head')), 'head', 0, 0)]
where the time goes in v1:
time: 395 us; the launch traced here: 394 us
  waiting for transfers between devices  178 us (45%)
  starting transfers between devices  62.1 us (16%)
  blocking collectives  46.5 us (12%)
  local copies, waits for them, and re-layouts  40.3 us (10%)
  matrix products  39.6 us (10%)
  other arithmetic  13.7 us (3%)
  between operations  13.7 us (3%)
    all_to_all x1, blocking collectives, on_device(): lax.all_to_all(outgoing[:, lo:hi], 'ctx', split_axis=0, concat_axis=0, ti...  46.5 us
    reduce_scatter x1, waiting for transfers between devices, on_device(): lax.psum_scatter(partial_proj, 'head', scatter_dimension=0, tiled=True)  45.2 us
    all_to_all x1, waiting for transfers between devices, on_device(): lax.all_to_all(outgoing[:, lo:hi], 'ctx', split_axis=0, concat_axis=0, ti...  34.8 us
    ppermute x7, waiting for transfers between devices, exclusive_scan(): got = lax.ppermute(window, axis, pairs)  31.2 us
    all_to_all x1, waiting for transfers between devices, on_device(): lax.all_to_all(jnp.stack([payload] * lax.axis_size('head')), 'head', 0, 0)  30.8 us
    ppermute x7, starting transfers between devices, exclusive_scan(): got = lax.ppermute(window, axis, pairs)  30.6 us
    reduce_scatter x2, waiting for transfers between devices, on_device(): lax.psum_scatter(partial_value, 'head', scatter_dimension=0, tiled=True)  25.5 us
    dot_general x2, matrix products, on_device(): jnp.einsum('rf,fgc->grc', activated, down, preferred_element_type=jnp.flo...  20.6 us
  transfers between devices with their start and end apart: 15, of which 10 were waited for; matrix products, arithmetic and copies ran while one was open for 12% of the time, Pallas kernels for 0%

profile of v1, /device:TPU:1, one launch (start us, length us, event | category | flops | bytes accessed | tf_op | source)
XLA Modules:
  0.0 394.2 jit_solution(13271470791700909378)
XLA Ops:
  13.1 6.0 %collective-permute-start.2 = (f32[4,136,128]{2,1,0:T(8,128)S(1)}, f32[4,136,128]{2,1,0:T(8,128)S(1)}, u32[]{:S(2)}, u32[]{:S(2)}) collective-permute-start(f32[4,136,128]{2,1,0:T(8,128)S(1)} %maximum_maximum_fusion), channel_id=1, source_target_pairs={{0,24},{8,32},{16,40},{24,48},{32,56},{40,64},{48,72},{56,80},{64,... | collective-permute-start | bytes 835592 | tf_op jit(solution)/shard_map/ppermute | solution.py:35
  24.3 6.0 %collective-permute-done.1 = f32[4,136,128]{2,1,0:T(8,128)S(1)} collective-permute-done((f32[4,136,128]{2,1,0:T(8,128)S(1)}, f32[4,136,128]{2,1,0:T(8,128)S(1)}, u32[]{:S(2)}, u32[]{:S(2)}) %collective-permute-start.1) | collective-permute-done | bytes 278560 | tf_op jit(solution)/shard_map/ppermute | solution.py:35
  36.4 5.3 %collective-permute-start.5 = (f32[4,136,128]{2,1,0:T(8,128)S(1)}, f32[4,136,128]{2,1,0:T(8,128)S(1)}, u32[]{:S(2)}, u32[]{:S(2)}) collective-permute-start(f32[4,136,128]{2,1,0:T(8,128)S(1)} %maximum_maximum_fusion.1), channel_id=1, source_target_pairs={{0,32},{8,40},{16,48},{24,56},{32,64},{40,72},{48,80},{56,88},{64,... | collective-permute-start | bytes 835592 | tf_op jit(solution)/shard_map/ppermute | solution.py:35
  44.9 6.0 %collective-permute-start.3 = (f32[4,136,128]{2,1,0:T(8,128)S(1)}, f32[4,136,128]{2,1,0:T(8,128)S(1)}, u32[]{:S(2)}, u32[]{:S(2)}) collective-permute-start(f32[4,136,128]{2,1,0:T(8,128)S(1)} %maximum_maximum_fusion.1), channel_id=1, source_target_pairs={{0,96},{8,104},{16,112},{24,120},{32,128},{40,136},{48,144},{56,15... | collective-permute-start | bytes 835592 | tf_op jit(solution)/shard_map/ppermute | solution.py:35
  52.5 15.9 %collective-permute-done.4 = f32[4,136,128]{2,1,0:T(8,128)S(1)} collective-permute-done((f32[4,136,128]{2,1,0:T(8,128)S(1)}, f32[4,136,128]{2,1,0:T(8,128)S(1)}, u32[]{:S(2)}, u32[]{:S(2)}) %collective-permute-start.4) | collective-permute-done | bytes 278560 | tf_op jit(solution)/shard_map/ppermute | solution.py:35
  69.0 5.8 %collective-permute-start.6 = (f32[4,136,128]{2,1,0:T(8,128)S(1)}, f32[4,136,128]{2,1,0:T(8,128)S(1)}, u32[]{:S(2)}, u32[]{:S(2)}) collective-permute-start(f32[4,136,128]{2,1,0:T(8,128)S(1)} %maximum_maximum_fusion.2), channel_id=1, source_target_pairs={{0,128},{8,136},{16,144},{24,152},{32,160},{40,168},{48,176},{56,1... | collective-permute-start | bytes 835592 | tf_op jit(solution)/shard_map/ppermute | solution.py:35
  76.3 4.3 %collective-permute-done.6 = f32[4,136,128]{2,1,0:T(8,128)S(1)} collective-permute-done((f32[4,136,128]{2,1,0:T(8,128)S(1)}, f32[4,136,128]{2,1,0:T(8,128)S(1)}, u32[]{:S(2)}, u32[]{:S(2)}) %collective-permute-start.6) | collective-permute-done | bytes 278560 | tf_op jit(solution)/shard_map/ppermute | solution.py:35
  82.3 4.6 %convolution_bitcast_fusion = f32[8,256,384]{2,1,0:T(8,128)} fusion(bf16[256,512,1]{0,1,2:T(8,128)(2,1)S(1)} %bitcast.163, bf16[8,384,512]{2,1,0:T(8,128)(2,1)} %bitcast.162), kind=kOutput, calls=%fused_computation.21 | convolution fusion | flops 805306368 | bytes 6553600 | tf_op jit(solution)/shard_map/tk,gck->gtc/dot_general | solution.py:97
  87.6 45.2 %reduce-scatter.4.cloned.1.call-done = f32[1,256,384]{2,1,0:T(8,128)} async-done(((f32[8,256,384]{2,1,0:T(8,128)}), f32[1,256,384]{2,1,0:T(8,128)}) %reduce-scatter.4.cloned.1.call-update) | async-done | bytes 393232 | tf_op jit(solution)/shard_map/reduce_scatter | solution.py:98
  135.8 5.0 %all-to-all-start = ((bf16[8,264,384]{2,1,0:T(8,128)(2,1)}), bf16[8,264,384]{2,1,0:T(8,128)(2,1)S(1)}, u32[]{:S(2)}, u32[]{:S(2)}) async-start(bf16[8,264,384]{2,1,0:T(8,128)(2,1)} %stack.2), calls=%async_computation.1 | async-start | bytes 3244032 | tf_op jit(solution)/shard_map/all_to_all | solution.py:109
  148.3 30.8 %all-to-all-done = bf16[8,264,384]{2,1,0:T(8,128)(2,1)S(1)} async-done(((bf16[8,264,384]{2,1,0:T(8,128)(2,1)}), bf16[8,264,384]{2,1,0:T(8,128)(2,1)S(1)}, u32[]{:S(2)}, u32[]{:S(2)}) %all-to-all-start) | async-done | bytes 1622048 | tf_op jit(solution)/shard_map/all_to_all | solution.py:109
  180.3 5.0 %gather_fusion = bf16[768,3072]{1,0:T(8,128)(2,1)} fusion(bf16[256,3072]{1,0:T(8,128)(2,1)S(1)} %multiply_convert_fusion, s32[1024]{0:T(1024)S(1)} %pad_clamp_fusion.1), kind=kCustom, calls=%fused_computation | custom fusion | bytes 9440256 | tf_op jit(solution)/shard_map/gather | solution.py:131
  192.0 10.7 %all-to-all-start.3 = ((bf16[32,12,3072]{2,1,0:T(8,128)(2,1)}), bf16[32,12,3072]{2,1,0:T(8,128)(2,1)}, u32[]{:S(2)}, u32[]{:S(2)}) async-start(bf16[32,12,3072]{2,1,0:T(8,128)(2,1)} %get-tuple-element.66), calls=%async_computation.5 | async-start | bytes 6291456 | tf_op jit(solution)/shard_map/all_to_all | solution.py:138
  202.8 4.9 %copy.136 = bf16[80,8,8,384]{3,2,1,0:T(8,128)(2,1)} copy(bf16[80,8,8,384]{3,1,2,0:T(8,128)(2,1)} %bitcast.159) | data formatting | bytes 7864320
  207.7 34.8 %all-to-all-done.3 = bf16[32,12,3072]{2,1,0:T(8,128)(2,1)} async-done(((bf16[32,12,3072]{2,1,0:T(8,128)(2,1)}), bf16[32,12,3072]{2,1,0:T(8,128)(2,1)}, u32[]{:S(2)}, u32[]{:S(2)}) %all-to-all-start.3) | async-done | bytes 2359328 | tf_op jit(solution)/shard_map/all_to_all | solution.py:138
  242.5 4.2 %reshape.316 = bf16[384,3072]{1,0:T(8,128)(2,1)} reshape(bf16[32,12,3072]{2,1,0:T(8,128)(2,1)} %all-to-all-done.3) | data formatting | bytes 4718592 | tf_op jit(solution)/shard_map/reshape | solution.py:141
  246.8 4.8 %fusion.4 = f32[384,640]{1,0:T(8,128)S(1)} fusion(bf16[384,3072]{1,0:T(8,128)(2,1)} %reshape.316, bf16[1,3072,640]{2,1,0:T(8,128)(2,1)} %param.31), kind=kOutput, calls=%fused_computation.9 | convolution fusion | flops 1509949440 | bytes 7274496 | tf_op jit(solution)/shard_map/dot_general | solution.py:142
  251.6 10.3 %convert_bitcast_fusion.1 = bf16[8,384,384]{2,1,0:T(8,128)(2,1)} fusion(bf16[640,8,384]{2,1,0:T(8,128)(2,1)} %bitcast.160, bf16[384,3072]{1,0:T(8,128)(2,1)} %reshape.316, bf16[1,3072,640]{2,1,0:T(8,128)(2,1)} %param.32, f32[384,640]{1,0:T(8,128)S(1)} %fusion.4), kind=kOutput, calls=%fused_computation.19 | convolution fusion | flops 3022553088 | bytes 13565952 | tf_op jit(solution)/shard_map/rf,fgc->grc/dot_general | solution.py:145
  262.0 46.5 %all_to_all.25 = bf16[32,12,3072]{2,1,0:T(8,128)(2,1)} all-to-all(bf16[32,12,3072]{2,1,0:T(8,128)(2,1)} %get-tuple-element.65), channel_id=1, replica_groups=mesh['ctx'=32,'head'=8] {'ctx'}, dimensions={0} | all-to-all | bytes 4718592 | tf_op jit(solution)/shard_map/all_to_all | solution.py:138
  312.7 4.8 %fusion.6 = f32[384,640]{1,0:T(8,128)S(1)} fusion(bf16[384,3072]{1,0:T(8,128)(2,1)} %reshape.314, bf16[1,3072,640]{2,1,0:T(8,128)(2,1)} %param.31), kind=kOutput, calls=%fused_computation.11 | convolution fusion | flops 1509949440 | bytes 7274496 | tf_op jit(solution)/shard_map/dot_general | solution.py:142
  317.6 10.3 %convert_bitcast_fusion.2 = bf16[8,384,384]{2,1,0:T(8,128)(2,1)} fusion(bf16[640,8,384]{2,1,0:T(8,128)(2,1)} %bitcast.161, bf16[384,3072]{1,0:T(8,128)(2,1)} %reshape.314, bf16[1,3072,640]{2,1,0:T(8,128)(2,1)} %param.32, f32[384,640]{1,0:T(8,128)S(1)} %fusion.6), kind=kOutput, calls=%fused_computation.20 | convolution fusion | flops 3022553088 | bytes 13565952 | tf_op jit(solution)/shard_map/rf,fgc->grc/dot_general | solution.py:145
  334.3 25.5 %reduce-scatter.6.cloned.1.call-done = bf16[1,384,384]{2,1,0:T(8,128)(2,1)} async-done(((bf16[8,384,384]{2,1,0:T(8,128)(2,1)}), bf16[1,384,384]{2,1,0:T(8,128)(2,1)}) %reduce-scatter.6.cloned.1.call-update) | async-done | bytes 294928 | tf_op jit(solution)/shard_map/reduce_scatter | solution.py:148
  361.5 11.7 %all-to-all-start.2 = ((bf16[32,12,384]{2,1,0:T(8,128)(2,1)}), bf16[32,12,384]{2,1,0:T(8,128)(2,1)S(1)}, u32[]{:S(2)}, u32[]{:S(2)}) async-start(bf16[32,12,384]{2,1,0:T(8,128)(2,1)} %reshape.315), calls=%async_computation.4 | async-start | bytes 786432 | tf_op jit(solution)/shard_map/all_to_all | solution.py:150
  373.5 9.9 %all-to-all-done.2 = bf16[32,12,384]{2,1,0:T(8,128)(2,1)S(1)} async-done(((bf16[32,12,384]{2,1,0:T(8,128)(2,1)}), bf16[32,12,384]{2,1,0:T(8,128)(2,1)S(1)}, u32[]{:S(2)}, u32[]{:S(2)}) %all-to-all-start.2) | async-done | bytes 294944 | tf_op jit(solution)/shard_map/all_to_all | solution.py:150
  (135 shorter events, 61.8 us)
Async XLA Ops:
  6.5 44.4 %copy-start = (bf16[256,512]{1,0:T(8,128)(2,1)S(1)}, bf16[256,512]{1,0:T(8,128)(2,1)}, u32[]{:S(2)}) copy-start(bf16[256,512]{1,0:T(8,128)(2,1)} %param.21) | copy-start | bytes 786436
  6.5 44.5 %copy-start.5 = (bf16[256,512]{1,0:T(8,128)(2,1)S(1)}, bf16[256,512]{1,0:T(8,128)(2,1)}, u32[]{:S(2)}) copy-start(bf16[256,512]{1,0:T(8,128)(2,1)} %param.23) | copy-start | bytes 786436
  6.5 75.8 %all-gather.2.cloned.1.call-start = ((), (), s32[]{:S(2)}) async-start(), calls=%async_computation.8 | async-start | bytes 3244032 | tf_op jit(solution)/shard_map/all_gather | solution.py:94
  7.3 125.6 %reduce-scatter.4.cloned.1.call-start = ((), (), s32[]{:S(2)}) async-start(), calls=%async_computation.9 | async-start | bytes 3538944 | tf_op jit(solution)/shard_map/reduce_scatter | solution.py:98
  10.8 25.5 %copy-start.10 = (f32[136]{0:T(256)}, f32[136]{0:T(256)S(1)}, u32[]{:S(2)}) copy-start(f32[136]{0:T(256)S(1)} %pad.23.clone) | copy-start | bytes 1636
  13.1 11.2 %collective-permute-start.2 = (f32[4,136,128]{2,1,0:T(8,128)S(1)}, f32[4,136,128]{2,1,0:T(8,128)S(1)}, u32[]{:S(2)}, u32[]{:S(2)}) collective-permute-start(f32[4,136,128]{2,1,0:T(8,128)S(1)} %maximum_maximum_fusion), channel_id=1, source_target_pairs={{0,24},{8,32},{16,40},{24,48},{32,56},{40,64},{48,72},{56,80},{64,... | collective-permute-start | bytes 835592 | tf_op jit(solution)/shard_map/ppermute | solution.py:35
  19.2 11.2 %collective-permute-start.1 = (f32[4,136,128]{2,1,0:T(8,128)S(1)}, f32[4,136,128]{2,1,0:T(8,128)S(1)}, u32[]{:S(2)}, u32[]{:S(2)}) collective-permute-start(f32[4,136,128]{2,1,0:T(8,128)S(1)} %maximum_maximum_fusion), channel_id=1, source_target_pairs={{0,8},{8,16},{16,24},{24,32},{32,40},{40,48},{48,56},{56,64},{64,7... | collective-permute-start | bytes 835592 | tf_op jit(solution)/shard_map/ppermute | solution.py:35
  21.1 13.3 %collective-permute-start = (f32[4,136,128]{2,1,0:T(8,128)S(1)}, f32[4,136,128]{2,1,0:T(8,128)S(1)}, u32[]{:S(2)}, u32[]{:S(2)}) collective-permute-start(f32[4,136,128]{2,1,0:T(8,128)S(1)} %maximum_maximum_fusion), channel_id=1, source_target_pairs={{0,16},{8,24},{16,32},{24,40},{32,48},{40,56},{48,64},{56,72},{64,... | collective-permute-start | bytes 835592 | tf_op jit(solution)/shard_map/ppermute | solution.py:35
  35.4 33.0 %copy-start.2 = (f32[4,136,128]{2,1,0:T(8,128)S(1)}, f32[4,136,128]{2,1,0:T(8,128)}, u32[]{:S(2)}) copy-start(f32[4,136,128]{2,1,0:T(8,128)} %constant.174.clone.1) | copy-start | bytes 835588
  36.0 8.9 %copy-start.7 = (f32[4,1,128]{2,1,0:T(1,128)}, f32[4,1,128]{2,1,0:T(1,128)S(1)}, u32[]{:S(2)}) copy-start(f32[4,1,128]{2,1,0:T(1,128)S(1)} %get-tuple-element.62) | copy-start | bytes 6148
  36.4 16.2 %collective-permute-start.5 = (f32[4,136,128]{2,1,0:T(8,128)S(1)}, f32[4,136,128]{2,1,0:T(8,128)S(1)}, u32[]{:S(2)}, u32[]{:S(2)}) collective-permute-start(f32[4,136,128]{2,1,0:T(8,128)S(1)} %maximum_maximum_fusion.1), channel_id=1, source_target_pairs={{0,32},{8,40},{16,48},{24,56},{32,64},{40,72},{48,80},{56,88},{64,... | collective-permute-start | bytes 835592 | tf_op jit(solution)/shard_map/ppermute | solution.py:35
  41.7 26.7 %collective-permute-start.4 = (f32[4,136,128]{2,1,0:T(8,128)S(1)}, f32[4,136,128]{2,1,0:T(8,128)S(1)}, u32[]{:S(2)}, u32[]{:S(2)}) collective-permute-start(f32[4,136,128]{2,1,0:T(8,128)S(1)} %maximum_maximum_fusion.1), channel_id=1, source_target_pairs={{0,64},{8,72},{16,80},{24,88},{32,96},{40,104},{48,112},{56,120},{... | collective-permute-start | bytes 835592 | tf_op jit(solution)/shard_map/ppermute | solution.py:35
  44.9 23.5 %collective-permute-start.3 = (f32[4,136,128]{2,1,0:T(8,128)S(1)}, f32[4,136,128]{2,1,0:T(8,128)S(1)}, u32[]{:S(2)}, u32[]{:S(2)}) collective-permute-start(f32[4,136,128]{2,1,0:T(8,128)S(1)} %maximum_maximum_fusion.1), channel_id=1, source_target_pairs={{0,96},{8,104},{16,112},{24,120},{32,128},{40,136},{48,144},{56,15... | collective-permute-start | bytes 835592 | tf_op jit(solution)/shard_map/ppermute | solution.py:35
  52.4 16.5 %copy-start.11 = (f32[136]{0:T(256)S(1)}, f32[136]{0:T(256)}, u32[]{:S(2)}) copy-start(f32[136]{0:T(256)} %copy-done.10) | copy-start | bytes 1636
  69.0 11.6 %collective-permute-start.6 = (f32[4,136,128]{2,1,0:T(8,128)S(1)}, f32[4,136,128]{2,1,0:T(8,128)S(1)}, u32[]{:S(2)}, u32[]{:S(2)}) collective-permute-start(f32[4,136,128]{2,1,0:T(8,128)S(1)} %maximum_maximum_fusion.2), channel_id=1, source_target_pairs={{0,128},{8,136},{16,144},{24,152},{32,160},{40,168},{48,176},{56,1... | collective-permute-start | bytes 835592 | tf_op jit(solution)/shard_map/ppermute | solution.py:35
  87.0 45.9 %copy-start.4 = (bf16[256,384]{1,0:T(8,128)(2,1)S(1)}, bf16[256,384]{1,0:T(8,128)(2,1)}, u32[]{:S(2)}) copy-start(bf16[256,384]{1,0:T(8,128)(2,1)} %param.27) | copy-start | bytes 589828
  87.6 53.2 %copy-start.9 = (s32[256,2]{0,1:T(2,128)S(1)}, s32[256,2]{0,1:T(2,128)}, u32[]{:S(2)}) copy-start(s32[256,2]{0,1:T(2,128)} %param.30) | copy-start | bytes 6148
  135.8 43.3 %all-to-all-start = ((bf16[8,264,384]{2,1,0:T(8,128)(2,1)}), bf16[8,264,384]{2,1,0:T(8,128)(2,1)S(1)}, u32[]{:S(2)}, u32[]{:S(2)}) async-start(bf16[8,264,384]{2,1,0:T(8,128)(2,1)} %stack.2), calls=%async_computation.1 | async-start | bytes 3244032 | tf_op jit(solution)/shard_map/all_to_all | solution.py:109
  192.0 50.5 %all-to-all-start.3 = ((bf16[32,12,3072]{2,1,0:T(8,128)(2,1)}), bf16[32,12,3072]{2,1,0:T(8,128)(2,1)}, u32[]{:S(2)}, u32[]{:S(2)}) async-start(bf16[32,12,3072]{2,1,0:T(8,128)(2,1)} %get-tuple-element.66), calls=%async_computation.5 | async-start | bytes 6291456 | tf_op jit(solution)/shard_map/all_to_all | solution.py:138
  202.7 125.2 %reduce-scatter.8.cloned.1.call-start = ((), (), s32[]{:S(2)}) async-start(), calls=%async_computation.11 | async-start | bytes 2654208 | tf_op jit(solution)/shard_map/reduce_scatter | solution.py:148
  261.9 97.8 %reduce-scatter.6.cloned.1.call-start = ((), (), s32[]{:S(2)}) async-start(), calls=%async_computation.10 | async-start | bytes 2654208 | tf_op jit(solution)/shard_map/reduce_scatter | solution.py:148
  327.9 5.8 %copy-start.6 = (bf16[3072,32]{0,1:T(8,128)(2,1)S(1)}, bf16[3072,32]{0,1:T(8,128)(2,1)}, u32[]{:S(2)}) copy-start(bf16[3072,32]{0,1:T(8,128)(2,1)} %param.29) | copy-start | bytes 589828
  329.7 31.8 %all-to-all-start.4 = ((bf16[32,12,384]{2,1,0:T(8,128)(2,1)}), bf16[32,12,384]{2,1,0:T(8,128)(2,1)S(1)}, u32[]{:S(2)}, u32[]{:S(2)}) async-start(bf16[32,12,384]{2,1,0:T(8,128)(2,1)} %reshape.317), calls=%async_computation.7 | async-start | bytes 786432 | tf_op jit(solution)/shard_map/all_to_all | solution.py:150
  361.5 21.9 %all-to-all-start.2 = ((bf16[32,12,384]{2,1,0:T(8,128)(2,1)}), bf16[32,12,384]{2,1,0:T(8,128)(2,1)S(1)}, u32[]{:S(2)}, u32[]{:S(2)}) async-start(bf16[32,12,384]{2,1,0:T(8,128)(2,1)} %reshape.315), calls=%async_computation.4 | async-start | bytes 786432 | tf_op jit(solution)/shard_map/all_to_all | solution.py:150
  (5 other events, 13.0 us)
Sparse Core Ops, SparseCore 0:
  9.9 61.5 all-gather.1
  87.1 45.7 reduce-scatter.3
  262.0 32.7 reduce-scatter.7
  328.0 31.6 reduce-scatter.5
